TPU v7x, 512 devices: a whole 4x4x16 slice. The times are simulated.
512 devices in a mesh: ctx: 16 (over z_lo, y), ch: 32 (over z_hi, x, core).
Axes of the slice: x: 4, y: 4, z: 16 (z_hi: 4, z_lo: 4; z = z_hi * 4 + z_lo), core: 2. Of those that a mesh axis runs over, the one named last changes fastest.
Arguments:
- bases_in: bfloat16 [6144, 4096], P('ctx', 'ch'), may hold values from -70 to 70
- norm_gain: float32 [4096], replicated, may hold values from 0.1 to 1.9
- w_in: bfloat16 [4096, 3, 4096], P(None, None, 'ch'), may hold values from -0.09375 to 0.09375
- feat_taps: float32 [3, 3, 4096], P(None, None, 'ch'), may hold values from -3.5 to 3.5
- long_filter: bfloat16 [4096, 128], P('ch'), may hold values from -0.5 to 0.5
- skip_gain: float32 [4096], P('ch'), may hold values from -4 to 4
- w_out: bfloat16 [4096, 4096], P('ch'), may hold values from -0.1875 to 0.1875
Outputs:
- mixed: bfloat16 [6144, 4096], P('ctx', 'ch')
All inputs are finite; a program needn't handle non-finite values.
Results may differ from a plain program's by a relative error of at most 0.02.
Values may be sent and summed in bfloat16 or wider, within the bound.
No kernel may reach another device: no remote copies, remote signals or barrier semaphores. Data moves between devices by JAX's collectives and lax.ppermute only.
A program may use at most 128 MiB of HBM per device.

v0:
```python
import jax
import jax.numpy as jnp
from jax import lax
from jax.sharding import PartitionSpec as P


def passed_along(value, axis, steps):
    count = lax.axis_size(axis)
    initial, last = (max(0, -steps), min(count, count - steps))
    return lax.ppermute(value, axis, [(source, source + steps) for source in range(initial, last)])


def featurize(extended, feat_taps, count):
    feat_len = feat_taps.shape[1]
    chans = feat_taps.shape[2]
    shaped = extended.reshape(extended.shape[0], 3, chans)
    feats = jnp.zeros((count, 3, chans), jnp.float32)
    for tap in range(feat_len):
        feats = feats + feat_taps[:, tap, :] * shaped[
            feat_len - 1 - tap : feat_len - 1 - tap + count
        ].astype(jnp.float32)
    return feats


def band_matrix(long_filter):
    chans, taps = long_filter.shape
    row_len = 3 * taps - 1
    reversed_taps = long_filter[:, ::-1]
    padded_row = jnp.concatenate(
        [
            jnp.zeros((chans, taps), jnp.bfloat16),
            reversed_taps,
            jnp.zeros((chans, taps - 1), jnp.bfloat16),
        ],
        axis=1,
    )
    tiled = jnp.broadcast_to(padded_row[:, None, :], (chans, taps, row_len)).reshape(
        chans, taps * row_len
    )
    skewed = tiled[:, taps - 1 : taps - 1 + taps * (row_len - 1)].reshape(chans, taps, row_len - 1)
    return skewed[:, :, : 2 * taps]


def shards(bases_in, norm_gain, w_in, feat_taps, long_filter, skip_gain, w_out):
    tok, chans = bases_in.shape
    width = norm_gain.shape[0]
    taps = long_filter.shape[1]
    feat_len = feat_taps.shape[1]
    w_flat = w_in.reshape(width, 3 * chans)
    whole = lax.all_gather(bases_in, "ch", axis=1, tiled=True)
    wide = whole.astype(jnp.float32)
    inverse = lax.rsqrt(jnp.mean(wide * wide, axis=1, keepdims=True) + 1e-05)
    normed = (wide * inverse * norm_gain).astype(jnp.bfloat16)
    mixed_in = jnp.dot(normed, w_flat, preferred_element_type=jnp.float32)
    projected = mixed_in.astype(jnp.bfloat16)
    earlier = passed_along(projected[tok - (feat_len - 1) :], "ctx", 1)
    feats = featurize(jnp.concatenate([earlier, projected], axis=0), feat_taps, tok)
    query = feats[:, 0, :]
    product = (feats[:, 1, :] * feats[:, 2, :]).astype(jnp.bfloat16)
    before = passed_along(product[tok - (taps - 1) :], "ctx", 1)
    extended = jnp.concatenate([jnp.zeros((1, chans), jnp.bfloat16), before, product], axis=0)
    toeplitz = band_matrix(long_filter)
    blocks = tok // taps
    older = extended[:tok].reshape(blocks, taps, chans)
    newer = extended[taps:].reshape(blocks, taps, chans)
    window = jnp.concatenate([older, newer], axis=1)
    filtered = jnp.einsum(
        "cij,bjc->bic", toeplitz, window, preferred_element_type=jnp.float32
    ).reshape(tok, chans)
    gated = (query * (filtered + skip_gain * product.astype(jnp.float32))).astype(jnp.bfloat16)
    terms = jnp.dot(gated, w_out, preferred_element_type=jnp.float32)
    return lax.psum_scatter(terms.astype(jnp.bfloat16), "ch", scatter_dimension=1, tiled=True)


def solution(mesh):
    in_specs = (
        P("ctx", "ch"),
        P(),
        P(None, None, "ch"),
        P(None, None, "ch"),
        P("ch", None),
        P("ch"),
        P("ch", None),
    )
    out_specs = P("ctx", "ch")
    return jax.shard_map(shards, mesh=mesh, in_specs=in_specs, out_specs=out_specs, check_vma=False)
```

profile of v0, /device:TPU:1, one launch (start us, length us, event | category | flops | bytes accessed | tf_op | source)
XLA Modules:
  0.0 345.5 jit_solution(9485300635172362352)
XLA Ops:
  6.5 0.0 copy-start
  6.5 0.0 copy-start.2
  6.5 0.0 copy-start.4
  6.5 0.0 all-gather.2.cloned.1.call-start
  6.5 0.7 all-gather.2.cloned.1.call-update
  7.3 0.0 reduce-scatter.4.cloned.1.call-start
  7.3 4.7 %copy.25 = bf16[4096,3,128]{0,2,1:T(8,128)(2,1)} copy(bf16[4096,3,128]{2,0,1:T(8,128)(2,1)} %param.9) | data formatting | bytes 6291456 | tf_op args[2]
  12.1 0.0 copy-done.2
  12.1 96.0 %all-gather.2.cloned.1.call-done = bf16[384,4096]{1,0:T(8,128)(2,1)} async-done(((bf16[384,128]{1,0:T(8,128)(2,1)}), bf16[384,4096]{1,0:T(8,128)(2,1)}) %all-gather.2.cloned.1.call-update) | async-done | bytes 3145744 | tf_op jit(solution)/shard_map/all_gather | solution.py:50
  108.1 2.6 fusion.2
  110.7 0.0 copy-start.1
  110.7 0.0 copy-done.4
  110.7 4.7 %fusion.9 = bf16[384,384]{1,0:T(8,128)(2,1)S(1)} fusion(bf16[4096,384]{0,1:T(8,128)(2,1)} %bitcast.38, bf16[384,4096]{1,0:T(8,128)(2,1)} %all-gather.2.cloned.1.call-done, f32[4096]{0:T(1024)S(1)} %copy-done.4, f32[384]{0:T(512)S(1)} %add_rsqrt_fusion), kind=kOutput, calls=%fused_computation.11 | convolution fusion | flops 1214398464 | bytes 6604288 | tf_op jit(solution)/shard_map/dot_general | solution.py:54
  115.4 2.9 collective-permute-start
  118.3 0.0 copy-done.1
  118.3 0.1 rev.3
  118.5 0.2 copy.26
  118.6 0.4 collective-permute-done
  119.0 0.1 fusion.16
  119.1 0.2 copy.28
  119.3 0.2 copy.27
  119.6 0.2 multiply_add_fusion
  119.8 0.1 slice_bitcast_fusion.1
  119.9 3.6 %collective-permute-start.1 = (bf16[127,128]{0,1:T(8,128)(2,1)S(1)}, bf16[127,128]{0,1:T(8,128)(2,1)S(1)}, u32[]{:S(2)}, u32[]{:S(2)}) collective-permute-start(bf16[127,128]{0,1:T(8,128)(2,1)S(1)} %slice_bitcast_fusion.1), channel_id=1, source_target_pairs={{0,32},{32,64},{64,96},{96,128},{128,160},{160,192},{192,224},{224... | collective-permute-start | bytes 97544 | tf_op jit(solution)/shard_map/ppermute | solution.py:10
  123.6 5.6 %broadcast_in_dim.21 = bf16[128,128,383]{2,1,0:T(8,128)(2,1)} broadcast(bf16[128,383]{1,0:T(8,128)(2,1)S(1)} %maximum_maximum_fusion), dimensions={0,2} | broadcast | bytes 12648192 | tf_op jit(solution)/shard_map/broadcast_in_dim | solution.py:37
  129.2 22.9 %reshape.49 = bf16[128,49024]{1,0:T(8,128)(2,1)} reshape(bf16[128,128,383]{2,1,0:T(8,128)(2,1)} %broadcast_in_dim.21) | data formatting | bytes 25100288 | tf_op jit(solution)/shard_map/reshape | solution.py:37
  152.1 11.6 %slice.68 = bf16[128,48896]{1,0:T(8,128)(2,1)} slice(bf16[128,49024]{1,0:T(8,128)(2,1)} %reshape.49), slice={[0:128], [127:49023]} | slice | bytes 25034752 | tf_op jit(solution)/shard_map/slice | solution.py:40
  163.8 33.8 %reshape.50 = bf16[128,128,382]{2,1,0:T(8,128)(2,1)} reshape(bf16[128,48896]{1,0:T(8,128)(2,1)} %slice.68) | data formatting | bytes 25034752 | tf_op jit(solution)/shard_map/reshape | solution.py:40
  197.6 0.0 copy-start.3
  197.6 0.1 copy.29
  197.7 0.1 copy.33
  197.9 0.0 collective-permute-done.1
  197.9 0.1 copy.30
  198.0 0.1 pad_maximum_fusion.1
  198.1 0.1 copy.32
  198.3 5.6 %fusion.12 = f32[3,128,128]{1,0,2:T(4,128)S(1)} fusion(bf16[128,128,382]{2,1,0:T(8,128)(2,1)} %reshape.50, bf16[3,128,128]{1,0,2:T(4,128)(2,1)S(1)} %copy.33, bf16[3,128,128]{1,0,2:T(4,128)(2,1)S(1)} %copy.32), kind=kOutput, calls=%fused_computation.12 | convolution fusion | flops 25559040 | bytes 8781824 | tf_op jit(solution)/shard_map/cij,bjc->bic/dot_general | solution.py:67
  203.9 0.1 copy.34
  204.1 0.1 copy.36
  204.2 0.0 copy-done
  204.2 0.0 copy-done.3
  204.2 2.8 convolution_convert_fusion
  207.0 4.6 %copy.38 = bf16[384,4096]{0,1:T(8,128)(2,1)} copy(bf16[384,4096]{1,0:T(8,128)(2,1)} %convolution_convert_fusion) | data formatting | bytes 6291456
  211.6 0.0 reduce-scatter.4.cloned.1.call-update
  211.7 125.4 %reduce-scatter.4.cloned.1.call-done = bf16[128,384]{1,0:T(8,128)(2,1)} async-done(((bf16[4096,384]{1,0:T(8,128)(2,1)}), bf16[128,384]{1,0:T(8,128)(2,1)}) %reduce-scatter.4.cloned.1.call-update) | async-done | bytes 98320
  337.0 1.6 copy.39
  (12 shorter events, 0.1 us)
Async XLA Ops:
  6.5 197.7 %copy-start = (bf16[128,4096]{1,0:T(8,128)(2,1)S(1)}, bf16[128,4096]{1,0:T(8,128)(2,1)}, u32[]{:S(2)}) copy-start(bf16[128,4096]{1,0:T(8,128)(2,1)} %param.13) | copy-start | bytes 3145732
  6.5 5.5 %copy-start.2 = (f32[3,3,128]{2,1,0:T(4,128)S(1)}, f32[3,3,128]{2,1,0:T(4,128)}, u32[]{:S(2)}) copy-start(f32[3,3,128]{2,1,0:T(4,128)} %param.10) | copy-start | bytes 13828
  6.5 104.1 %copy-start.4 = (f32[4096]{0:T(1024)S(1)}, f32[4096]{0:T(1024)}, u32[]{:S(2)}) copy-start(f32[4096]{0:T(1024)} %param.8) | copy-start | bytes 49156
  6.5 101.5 %all-gather.2.cloned.1.call-start = ((), (), s32[]{:S(2)}) async-start(), calls=%async_computation.1 | async-start | bytes 3244032 | tf_op jit(solution)/shard_map/all_gather | solution.py:50
  7.3 329.8 %reduce-scatter.4.cloned.1.call-start = ((), (), s32[]{:S(2)}) async-start(), calls=%async_computation.2 | async-start | bytes 3244032
  110.7 7.7 %copy-start.1 = (bf16[128,128]{1,0:T(8,128)(2,1)S(1)}, bf16[128,128]{1,0:T(8,128)(2,1)}, u32[]{:S(2)}) copy-start(bf16[128,128]{1,0:T(8,128)(2,1)} %param.11) | copy-start | bytes 98308
  115.4 3.6 %collective-permute-start = (bf16[2,384]{1,0:T(2,128)(2,1)S(1)}, bf16[2,384]{1,0:T(2,128)(2,1)S(1)}, u32[]{:S(2)}, u32[]{:S(2)}) collective-permute-start(bf16[2,384]{1,0:T(2,128)(2,1)S(1)} %slice.60), channel_id=1, source_target_pairs={{0,32},{32,64},{64,96},{96,128},{128,160},{160,192},{192,224},{224... | collective-permute-start | bytes 4616 | tf_op jit(solution)/shard_map/ppermute | solution.py:10
  119.9 77.9 %collective-permute-start.1 = (bf16[127,128]{0,1:T(8,128)(2,1)S(1)}, bf16[127,128]{0,1:T(8,128)(2,1)S(1)}, u32[]{:S(2)}, u32[]{:S(2)}) collective-permute-start(bf16[127,128]{0,1:T(8,128)(2,1)S(1)} %slice_bitcast_fusion.1), channel_id=1, source_target_pairs={{0,32},{32,64},{64,96},{96,128},{128,160},{160,192},{192,224},{224... | collective-permute-start | bytes 97544 | tf_op jit(solution)/shard_map/ppermute | solution.py:10
  197.6 6.6 %copy-start.3 = (f32[128]{0:T(128)S(1)}, f32[128]{0:T(128)}, u32[]{:S(2)}) copy-start(f32[128]{0:T(128)} %param.12) | copy-start | bytes 1540
Sparse Core Ops, SparseCore 0:
  10.4 97.6 all-gather.1
  211.8 125.1 reduce-scatter.3
where the time goes:
time: 346 us; the launch traced here: 345 us
  waiting for transfers between devices  222 us (64%)
  local copies, waits for them, and re-layouts  86.7 us (25%)
  between operations  13.6 us (4%)
  matrix products  13.1 us (4%)
  starting transfers between devices  6.54 us (2%)
    unnamed x3, waiting for transfers between devices  126 us
    all_gather x1, waiting for transfers between devices, shards(): whole = lax.all_gather(bases_in, 'ch', axis=1, tiled=True)  96 us
    reshape x1, local copies, waits for them, and re-layouts, band_matrix(): tiled[:, taps - 1:taps - 1 + taps * (row_len - 1)]  33.8 us
    reshape x1, local copies, waits for them, and re-layouts, band_matrix(): jnp.broadcast_to(padded_row[:, None, :], (chans, taps, row_len))  22.9 us
    slice x1, local copies, waits for them, and re-layouts, band_matrix(): tiled[:, taps - 1:taps - 1 + taps * (row_len - 1)]  11.6 us
    unnamed x15, local copies, waits for them, and re-layouts  11 us
  transfers between devices with their start and end apart: 4, of which 3 were waited for; matrix products, arithmetic and copies ran while one was open for 23% of the time, Pallas kernels for 0%

commit v1 on v0

--- a/solution.py
+++ b/solution.py
@@ -47,7 +47,9 @@
     taps = long_filter.shape[1]
     feat_len = feat_taps.shape[1]
     w_flat = w_in.reshape(width, 3 * chans)
-    whole = lax.all_gather(bases_in, "ch", axis=1, tiled=True)
+    whole = jnp.concatenate(
+        lax.all_to_all(jnp.stack(lax.psum(1, "ch") * [bases_in], 0), "ch", 0, 0), 1
+    )
     wide = whole.astype(jnp.float32)
     inverse = lax.rsqrt(jnp.mean(wide * wide, axis=1, keepdims=True) + 1e-05)
     normed = (wide * inverse * norm_gain).astype(jnp.bfloat16)

time: 346 us -> 412 us (1.19)
  waiting for transfers between devices: 222 us -> 264 us
  starting transfers between devices: 6.54 us -> 26.3 us
    all_to_all x0 -> x1, waiting for transfers between devices: none -> 139 us  [shards(): lax.all_to_all(jnp.stack(lax.psum(1, 'ch') * [bases_in], 0), 'ch', 0, 0)]
    all_gather x1 -> x0, waiting for transfers between devices: 96 us -> none  [shards(): whole = lax.all_gather(bases_in, 'ch', axis=1, tiled=True)]
    all_to_all x0 -> x1, starting transfers between devices: none -> 19.3 us  [shards(): lax.all_to_all(jnp.stack(lax.psum(1, 'ch') * [bases_in], 0), 'ch', 0, 0)]
    unnamed x15 -> x18, local copies, waits for them, and re-layouts: 11 us -> 12.6 us
    unnamed x3 -> x2, waiting for transfers between devices: 126 us -> 125 us
  transfers between devices with their start and end apart: 4 -> 4, of which waited for: 3 -> 3; matrix products, arithmetic and copies ran while one was open for 23% -> 19% of each run, Pallas kernels for 0% -> 0%
where the time goes in v1:
time: 412 us; the launch traced here: 410 us
  waiting for transfers between devices  264 us (64%)
  local copies, waits for them, and re-layouts  90.4 us (22%)
  starting transfers between devices  26.3 us (6%)
  between operations  13.6 us (3%)
  matrix products  10.2 us (2%)
  other arithmetic  5.67 us (1%)
    all_to_all x1, waiting for transfers between devices, shards(): lax.all_to_all(jnp.stack(lax.psum(1, 'ch') * [bases_in], 0), 'ch', 0, 0)  139 us
    unnamed x2, waiting for transfers between devices  125 us
    reshape x1, local copies, waits for them, and re-layouts, band_matrix(): tiled[:, taps - 1:taps - 1 + taps * (row_len - 1)]  33.8 us
    reshape x1, local copies, waits for them, and re-layouts, band_matrix(): jnp.broadcast_to(padded_row[:, None, :], (chans, taps, row_len))  22.9 us
    all_to_all x1, starting transfers between devices, shards(): lax.all_to_all(jnp.stack(lax.psum(1, 'ch') * [bases_in], 0), 'ch', 0, 0)  19.3 us
    unnamed x18, local copies, waits for them, and re-layouts  12.6 us
    slice x1, local copies, waits for them, and re-layouts, band_matrix(): tiled[:, taps - 1:taps - 1 + taps * (row_len - 1)]  11.6 us
  transfers between devices with their start and end apart: 4, of which 3 were waited for; matrix products, arithmetic and copies ran while one was open for 19% of the time, Pallas kernels for 0%

profile of v1, /device:TPU:1, one launch (start us, length us, event | category | flops | bytes accessed | tf_op | source)
XLA Modules:
  0.0 410.4 jit_solution(1631463012941711661)
XLA Ops:
  6.5 0.0 copy-start
  6.5 1.1 copy.26
  7.6 2.2 stack.2
  9.8 19.3 %all-to-all-start = ((bf16[32,384,128]{1,2,0:T(8,128)(2,1)}), bf16[32,384,128]{1,2,0:T(8,128)(2,1)}, u32[]{:S(2)}, u32[]{:S(2)}) async-start(bf16[32,384,128]{1,2,0:T(8,128)(2,1)} %stack.2), calls=%async_computation | async-start | bytes 6291456 | tf_op jit(solution)/shard_map/all_to_all | solution.py:51
  29.1 0.0 copy-start.4
  29.1 0.0 reduce-scatter.4.cloned.1.call-start
  29.1 4.9 %copy.27 = bf16[4096,3,128]{0,2,1:T(8,128)(2,1)} copy(bf16[4096,3,128]{2,0,1:T(8,128)(2,1)} %param.9) | data formatting | bytes 6291456 | tf_op args[2]
  34.0 0.0 copy-done.4
  34.0 0.0 copy-start.3
  34.0 139.0 %all-to-all-done = bf16[32,384,128]{1,2,0:T(8,128)(2,1)} async-done(((bf16[32,384,128]{1,2,0:T(8,128)(2,1)}), bf16[32,384,128]{1,2,0:T(8,128)(2,1)}, u32[]{:S(2)}, u32[]{:S(2)}) %all-to-all-start) | async-done | bytes 3145760 | tf_op jit(solution)/shard_map/all_to_all | solution.py:51
  173.0 2.7 fusion.2
  175.7 0.0 copy-done.3
  175.7 0.0 copy-start.1
  175.7 2.5 fusion.4
  178.2 0.3 copy-done.1
  178.6 0.0 copy-start.2
  178.6 1.8 convolution_convert_fusion.1
  180.4 3.2 collective-permute-start
  183.6 0.0 copy-done.2
  183.6 0.1 rev.3
  183.8 0.2 copy.28
  184.0 0.4 collective-permute-done
  184.3 0.1 fusion.9
  184.4 0.2 copy.30
  184.7 0.2 copy.29
  184.9 0.2 multiply_add_fusion
  185.2 0.1 slice_bitcast_fusion.1
  185.2 3.8 collective-permute-start.1
  189.1 5.6 %broadcast_in_dim.21 = bf16[128,128,383]{2,1,0:T(8,128)(2,1)} broadcast(bf16[128,383]{1,0:T(8,128)(2,1)S(1)} %maximum_maximum_fusion), dimensions={0,2} | broadcast | bytes 12648192 | tf_op jit(solution)/shard_map/broadcast_in_dim | solution.py:37
  194.7 22.9 %reshape.64 = bf16[128,49024]{1,0:T(8,128)(2,1)} reshape(bf16[128,128,383]{2,1,0:T(8,128)(2,1)} %broadcast_in_dim.21) | data formatting | bytes 25100288 | tf_op jit(solution)/shard_map/reshape | solution.py:37
  217.6 11.6 %slice.68 = bf16[128,48896]{1,0:T(8,128)(2,1)} slice(bf16[128,49024]{1,0:T(8,128)(2,1)} %reshape.64), slice={[0:128], [127:49023]} | slice | bytes 25034752 | tf_op jit(solution)/shard_map/slice | solution.py:40
  229.3 33.8 %reshape.65 = bf16[128,128,382]{2,1,0:T(8,128)(2,1)} reshape(bf16[128,48896]{1,0:T(8,128)(2,1)} %slice.68) | data formatting | bytes 25034752 | tf_op jit(solution)/shard_map/reshape | solution.py:40
  263.1 0.1 copy.31
  263.2 0.1 copy.35
  263.4 0.0 collective-permute-done.1
  263.4 0.1 copy.32
  263.5 0.1 pad_maximum_fusion.1
  263.6 0.1 copy.34
  263.8 0.0 copy-start.5
  263.8 5.6 %fusion.5 = f32[3,128,128]{1,0,2:T(4,128)S(1)} fusion(bf16[128,128,382]{2,1,0:T(8,128)(2,1)} %reshape.65, bf16[3,128,128]{1,0,2:T(4,128)(2,1)S(1)} %copy.35, bf16[3,128,128]{1,0,2:T(4,128)(2,1)S(1)} %copy.34), kind=kOutput, calls=%fused_computation.9 | convolution fusion | flops 25559040 | bytes 8781824 | tf_op jit(solution)/shard_map/cij,bjc->bic/dot_general | solution.py:69
  269.4 0.1 copy.36
  269.6 0.1 copy.38
  269.7 0.0 copy-done
  269.7 0.0 copy-done.5
  269.7 2.8 convolution_convert_fusion
  272.5 4.6 %copy.40 = bf16[384,4096]{0,1:T(8,128)(2,1)} copy(bf16[384,4096]{1,0:T(8,128)(2,1)} %convolution_convert_fusion) | data formatting | bytes 6291456
  277.1 0.0 reduce-scatter.4.cloned.1.call-update
  277.2 124.7 %reduce-scatter.4.cloned.1.call-done = bf16[128,384]{1,0:T(8,128)(2,1)} async-done(((bf16[4096,384]{1,0:T(8,128)(2,1)}), bf16[128,384]{1,0:T(8,128)(2,1)}) %reduce-scatter.4.cloned.1.call-update) | async-done | bytes 98320
  401.9 1.6 copy.41
  (12 shorter events, 0.1 us)
Async XLA Ops:
  6.5 263.2 %copy-start = (bf16[128,4096]{1,0:T(8,128)(2,1)S(1)}, bf16[128,4096]{1,0:T(8,128)(2,1)}, u32[]{:S(2)}) copy-start(bf16[128,4096]{1,0:T(8,128)(2,1)} %param.13) | copy-start | bytes 3145732
  9.8 163.2 %all-to-all-start = ((bf16[32,384,128]{1,2,0:T(8,128)(2,1)}), bf16[32,384,128]{1,2,0:T(8,128)(2,1)}, u32[]{:S(2)}, u32[]{:S(2)}) async-start(bf16[32,384,128]{1,2,0:T(8,128)(2,1)} %stack.2), calls=%async_computation | async-start | bytes 6291456 | tf_op jit(solution)/shard_map/all_to_all | solution.py:51
  29.1 4.9 %copy-start.4 = (f32[3,3,128]{2,1,0:T(4,128)S(1)}, f32[3,3,128]{2,1,0:T(4,128)}, u32[]{:S(2)}) copy-start(f32[3,3,128]{2,1,0:T(4,128)} %param.10) | copy-start | bytes 13828
  29.1 372.8 %reduce-scatter.4.cloned.1.call-start = ((), (), s32[]{:S(2)}) async-start(), calls=%async_computation.2 | async-start | bytes 3244032
  34.0 141.7 %copy-start.3 = (f32[4096]{0:T(1024)S(1)}, f32[4096]{0:T(1024)}, u32[]{:S(2)}) copy-start(f32[4096]{0:T(1024)} %param.8) | copy-start | bytes 49156
  175.7 2.8 copy-start.1
  178.6 5.1 %copy-start.2 = (bf16[128,128]{1,0:T(8,128)(2,1)S(1)}, bf16[128,128]{1,0:T(8,128)(2,1)}, u32[]{:S(2)}) copy-start(bf16[128,128]{1,0:T(8,128)(2,1)} %param.11) | copy-start | bytes 98308
  180.4 3.9 collective-permute-start
  185.2 78.1 %collective-permute-start.1 = (bf16[127,128]{0,1:T(8,128)(2,1)S(1)}, bf16[127,128]{0,1:T(8,128)(2,1)S(1)}, u32[]{:S(2)}, u32[]{:S(2)}) collective-permute-start(bf16[127,128]{0,1:T(8,128)(2,1)S(1)} %slice_bitcast_fusion.1), channel_id=1, source_target_pairs={{0,32},{32,64},{64,96},{96,128},{128,160},{160,192},{192,224},{224... | collective-permute-start | bytes 97544 | tf_op jit(solution)/shard_map/ppermute | solution.py:10
  263.8 6.0 %copy-start.5 = (f32[128]{0:T(128)S(1)}, f32[128]{0:T(128)}, u32[]{:S(2)}) copy-start(f32[128]{0:T(128)} %param.12) | copy-start | bytes 1540
Sparse Core Ops, SparseCore 0:
  277.3 124.5 reduce-scatter.3
